TPU v7x, 256 devices: a whole 4x4x8 slice. The times are simulated.
256 devices in a mesh: tile: 128 (over z, x, y), chan: 2 (over core).
Axes of the slice: x: 4, y: 4, z: 8, core: 2. Of those that a mesh axis runs over, the one named last changes fastest.
Arguments:
- jacobian: bfloat16 [1024, 616, 411], P('tile', 'chan'), may hold values from -0.3125 to 0.3125
- r_inverse: bfloat16 [616, 616], P('chan'), as said below
- innovation: bfloat16 [1024, 616], P('tile', 'chan'), may hold values from -6 to 6
- increments: bfloat16 [2048, 128, 411], P('tile'), may hold values from -6 to 6
- owner_offset: int32 [1024, 1], P('tile'), may hold values from 0 to 3; in each aligned block of 8 rows (0 to 7, 8 to 15, ...) at most 3 rows name the same one
- column_slot: int32 [1024], P('tile'), may hold values from 0 to 15
- foot_counts: int32 [128], P('tile'), may hold values from 1 to 8, as said below
Outputs:
- gradient: bfloat16 [2048, 128, 411], P('tile')
Inputs may be any that keep to these rules, and one draw needn't show every extreme that they name: r_inverse is symmetric. `owner_offset`: the 8 footprints of one tile name each value at most 3 times, and some tile names some value exactly 3 times. `foot_counts`: each count is 8 divided by 1, 2, 4 or 8; some tile has 8.
All inputs are finite; a program needn't handle non-finite values.
Results may differ from a plain program's by a relative error of at most 0.0052.
Values may be sent and summed in bfloat16 or wider, within the bound.
No kernel may reach another device: no remote copies, remote signals or barrier semaphores. Data moves between devices by JAX's collectives and lax.ppermute only.
A program may use at most 64 MiB of HBM per device.

v0:
```python
import jax
import jax.numpy as jnp
from jax import lax
from jax.sharding import PartitionSpec as P

SPAN = 4
CAP = 3
group_rows = 8


def passed_along(value, axis, by):
    count = lax.axis_size(axis)
    return lax.ppermute(value, axis, [(i, (i + by) % count) for i in range(count)])


def on_device(jacobian, r_inverse, innovation, increments, owner_offset, column_slot, foot_counts):
    foot = jacobian.shape[0]
    state = jacobian.shape[2]
    columns = increments.shape[0]
    members = increments.shape[1]
    capacity = CAP
    slots_total = SPAN * capacity
    offset = owner_offset[:, 0]
    order = jnp.arange(foot, dtype=jnp.int32)
    earlier = (offset[:, None] == offset[None, :]) & (order[None, :] < order[:, None])
    rank = jnp.sum(earlier.astype(jnp.int32), axis=1)
    place = offset * capacity + rank
    select = place[None, :] == jnp.arange(slots_total, dtype=jnp.int32)[:, None]
    request = jnp.sum(jnp.where(select, column_slot[None, :], 0), axis=1)
    jac_all, innov_all, r_all = (jacobian, innovation, r_inverse)
    fetched_parts = []
    for neighbor_rank in range(SPAN):
        wanted = request[neighbor_rank * capacity : (neighbor_rank + 1) * capacity]
        if neighbor_rank == 1:
            fetched_parts.append(jnp.take(increments, wanted, axis=0))
        else:
            asked = passed_along(wanted, "tile", neighbor_rank - 1)
            picked = jnp.take(increments, asked, axis=0)
            fetched_parts.append(passed_along(picked, "tile", 1 - neighbor_rank))
    fetched = jnp.concatenate(fetched_parts, axis=0)
    column_state = jnp.take(fetched, place, axis=0)
    count = foot_counts[0]
    block_total = (count + group_rows - 1) // group_rows
    adjoint_buf = jnp.zeros((foot, members, state), jnp.bfloat16)

    def one_block(block_index, buf):
        start = block_index * group_rows
        evolved = jnp.einsum(
            "fks,fms->fmk", jac_all, column_state, preferred_element_type=jnp.float32
        )
        departure = (evolved - innov_all.astype(jnp.float32)[:, None, :]).astype(jnp.bfloat16)
        all_channels = lax.all_gather(departure, "chan", axis=2, tiled=True)
        weighted = jnp.einsum(
            "fmk,ik->fmi", all_channels, r_all, preferred_element_type=jnp.float32
        )
        weighted = weighted.astype(jnp.bfloat16)
        partial_adj = jnp.einsum(
            "fks,fmk->fms", jac_all, weighted, preferred_element_type=jnp.float32
        )
        summed = lax.psum(partial_adj, "chan")
        live = start + jnp.arange(group_rows, dtype=jnp.int32) < count
        summed = jnp.where(live[:, None, None], summed, jnp.zeros_like(summed)).astype(jnp.bfloat16)
        return summed

    adjoint_buf = lax.fori_loop(0, block_total, one_block, adjoint_buf)
    flat = adjoint_buf.reshape(foot, members * state)
    packed = jnp.dot(select.astype(jnp.bfloat16), flat, preferred_element_type=jnp.float32).astype(
        jnp.bfloat16
    )
    received_parts = []
    slot_parts = []
    for neighbor_rank in range(SPAN):
        piece = packed[neighbor_rank * capacity : (neighbor_rank + 1) * capacity]
        wanted = request[neighbor_rank * capacity : (neighbor_rank + 1) * capacity]
        if neighbor_rank == 1:
            received_parts.append(piece)
            slot_parts.append(wanted)
        else:
            moved, moved_slots = passed_along((piece, wanted), "tile", neighbor_rank - 1)
            received_parts.append(moved)
            slot_parts.append(moved_slots)
    received = jnp.concatenate(received_parts, axis=0)
    got_slots = jnp.concatenate(slot_parts, axis=0)
    assign = (got_slots[None, :] == jnp.arange(columns, dtype=jnp.int32)[:, None]).astype(
        jnp.bfloat16
    )
    gradient = jnp.dot(assign, received, preferred_element_type=jnp.float32).astype(jnp.bfloat16)
    gradient = gradient.reshape(columns, members, state)
    return gradient


def solution(mesh):
    in_specs = (
        P("tile", "chan", None),
        P("chan", None),
        P("tile", "chan"),
        P("tile", None, None),
        P("tile", None),
        P("tile"),
        P("tile"),
    )
    out_specs = P("tile", None, None)
    return jax.shard_map(
        on_device, mesh=mesh, in_specs=in_specs, out_specs=out_specs, check_vma=False
    )
```

profile of v0, /device:TPU:8, one launch (start us, length us, event | category | flops | bytes accessed | tf_op | source)
XLA Modules:
  0.0 157.8 jit_solution(7195260682323156579)
XLA Ops:
  6.5 0.0 copy-start
  6.5 0.0 all-gather.2.cloned.1.call-start
  6.5 1.0 convert_reduce_fusion
  7.5 0.7 multiply_add_fusion
  8.2 0.7 select_reduce_fusion
  8.9 0.1 fusion.22
  9.0 2.2 %collective-permute-start = (s32[3]{0:T(128)S(1)}, s32[3]{0:T(128)S(1)}, u32[]{:S(2)}, u32[]{:S(2)}) collective-permute-start(s32[3]{0:T(128)S(1)} %get-tuple-element.221), channel_id=1, source_target_pairs={{0,254},{2,0},{4,2},{6,4},{8,6},{10,8},{12,10},{14,12},{16,14},{18... | collective-permute-start | bytes 44 | tf_op jit(solution)/shard_map/ppermute | solution.py:13
  11.2 0.0 collective-permute-start.1
  11.2 4.3 %collective-permute-start.2 = (s32[3]{0:T(128)S(1)}, s32[3]{0:T(128)S(1)}, u32[]{:S(2)}, u32[]{:S(2)}) collective-permute-start(s32[3]{0:T(128)S(1)} %get-tuple-element.219), channel_id=1, source_target_pairs={{0,4},{2,6},{4,8},{6,10},{8,12},{10,14},{12,16},{14,18},{16,20},{1... | collective-permute-start | bytes 44 | tf_op jit(solution)/shard_map/ppermute | solution.py:13
  15.4 0.1 compare_and_fusion.2
  15.5 0.7 and_bitcast_fusion
  16.2 0.0 copy-start.1
  16.2 4.5 %copy.26 = bf16[8,308,411]{1,2,0:T(8,128)(2,1)} copy(bf16[8,308,411]{2,0,1:T(8,128)(2,1)} %param.11) | data formatting | bytes 4050816 | tf_op args[0]
  20.7 0.0 copy-done.1
  20.8 0.0 copy-done
  20.8 2.5 %gather_fusion.2 = bf16[3,128,411]{1,0,2:T(4,128)(2,1)S(1)} fusion(bf16[16,128,411]{1,0,2:T(8,128)(2,1)S(1)} %copy-done, s32[1024]{0:T(1024)S(1)} %pad_clamp_fusion.3), kind=kCustom, calls=%fused_computation.1.clone | custom fusion | bytes 631308 | tf_op jit(solution)/shard_map/jit(_take)/gather | solution.py:35
  23.2 0.0 collective-permute-done
  23.3 2.5 %gather_fusion.1 = bf16[3,128,411]{1,0,2:T(4,128)(2,1)S(1)} fusion(bf16[16,128,411]{1,0,2:T(8,128)(2,1)S(1)} %copy-done, s32[1024]{0:T(1024)S(1)} %pad_clamp_fusion.4), kind=kCustom, calls=%fused_computation.clone | custom fusion | bytes 631308 | tf_op jit(solution)/shard_map/jit(_take)/gather | solution.py:38
  25.7 1.0 broadcast_select_fusion.3
  26.8 0.0 collective-permute-start.3
  26.8 0.0 collective-permute-done.1
  26.8 2.5 %gather_fusion.3 = bf16[3,128,411]{1,0,2:T(4,128)(2,1)S(1)} fusion(bf16[16,128,411]{1,0,2:T(8,128)(2,1)S(1)} %copy-done, s32[1024]{0:T(1024)S(1)} %pad_clamp_fusion.2), kind=kCustom, calls=%fused_computation.2.clone | custom fusion | bytes 631308 | tf_op jit(solution)/shard_map/jit(_take)/gather | solution.py:38
  29.3 1.0 broadcast_select_fusion.1
  30.3 4.5 %collective-permute-start.4 = (bf16[3,128,411]{1,0,2:T(4,128)(2,1)}, bf16[3,128,411]{1,0,2:T(4,128)(2,1)S(1)}, u32[]{:S(2)}, u32[]{:S(2)}) collective-permute-start(bf16[3,128,411]{1,0,2:T(4,128)(2,1)} %broadcast_select_fusion.1), channel_id=1, source_target_pairs={{0,254},{2,0},{4,2},{6,4},{8,6},{10,8},{12,10},{14,12},{16,14},{18... | collective-permute-start | bytes 946952 | tf_op jit(solution)/shard_map/ppermute | solution.py:13
  34.8 0.0 collective-permute-done.2
  34.8 2.5 %gather_fusion.4 = bf16[3,128,411]{1,0,2:T(4,128)(2,1)S(1)} fusion(bf16[16,128,411]{1,0,2:T(8,128)(2,1)S(1)} %copy-done, s32[1024]{0:T(1024)S(1)} %pad_clamp_fusion.1), kind=kCustom, calls=%fused_computation.3.clone | custom fusion | bytes 631308 | tf_op jit(solution)/shard_map/jit(_take)/gather | solution.py:38
  37.3 0.2 broadcast_select_fusion
  37.5 8.4 %collective-permute-start.5 = (bf16[3,128,411]{1,0,2:T(4,128)(2,1)S(1)}, bf16[3,128,411]{1,0,2:T(4,128)(2,1)S(1)}, u32[]{:S(2)}, u32[]{:S(2)}) collective-permute-start(bf16[3,128,411]{1,0,2:T(4,128)(2,1)S(1)} %broadcast_select_fusion), channel_id=1, source_target_pairs={{0,252},{2,254},{4,0},{6,2},{8,4},{10,6},{12,8},{14,10},{16,12},{1... | collective-permute-start | bytes 946952 | tf_op jit(solution)/shard_map/ppermute | solution.py:13
  45.9 0.2 broadcast_select_fusion.2
  46.1 0.0 collective-permute-done.3
  46.1 6.7 %collective-permute-done.4 = bf16[3,128,411]{1,0,2:T(4,128)(2,1)S(1)} collective-permute-done((bf16[3,128,411]{1,0,2:T(4,128)(2,1)}, bf16[3,128,411]{1,0,2:T(4,128)(2,1)S(1)}, u32[]{:S(2)}, u32[]{:S(2)}) %collective-permute-start.4) | collective-permute-done | bytes 315680 | tf_op jit(solution)/shard_map/ppermute | solution.py:13
  52.8 4.7 %collective-permute-done.5 = bf16[3,128,411]{1,0,2:T(4,128)(2,1)S(1)} collective-permute-done((bf16[3,128,411]{1,0,2:T(4,128)(2,1)S(1)}, bf16[3,128,411]{1,0,2:T(4,128)(2,1)S(1)}, u32[]{:S(2)}, u32[]{:S(2)}) %collective-permute-start.5) | collective-permute-done | bytes 315680 | tf_op jit(solution)/shard_map/ppermute | solution.py:13
  57.5 1.4 pad_maximum_fusion
  58.8 0.3 copy.22
  59.2 1.6 gather_fusion
  60.7 3.3 %fusion.7 = bf16[8,128,308]{1,2,0:T(8,128)(2,1)S(1)} fusion(bf16[8,308,411]{1,2,0:T(8,128)(2,1)} %copy.26, bf16[8,128,411]{1,2,0:T(8,128)(2,1)} %gather_fusion, pred[8]{0:T(512)(128)(4,1)S(1)} %get-tuple-element.210, f32[8,308]{1,0:T(8,128)S(1)} %convert_element_type.46), kind=kOutput, calls=%fused_computation.18 | convolution fusion | flops 260303872 | bytes 3507784 | tf_op jit(solution)/shard_map/while/body/fks,fms->fmk/dot_general | solution.py:48
  64.0 0.9 copy.24
  64.9 0.0 all-gather.2.cloned.1.call-update
  65.6 15.6 %all-gather.2.cloned.1.call-done = bf16[8,128,616]{1,0,2:T(8,128)(2,1)} async-done(((bf16[8,128,308]{1,0,2:T(8,128)(2,1)}), bf16[8,128,616]{1,0,2:T(8,128)(2,1)}) %all-gather.2.cloned.1.call-update) | async-done | bytes 1261584 | tf_op jit(solution)/shard_map/while/body/all_gather | solution.py:52
  81.2 3.6 %fusion.8 = f32[8,128,411]{1,2,0:T(8,128)S(1)} fusion(bf16[8,308,411]{1,2,0:T(8,128)(2,1)} %copy.26, bf16[8,128,616]{1,0,2:T(8,128)(2,1)} %all-gather.2.cloned.1.call-done, bf16[308,616]{1,0:T(8,128)(2,1)} %param.12), kind=kOutput, calls=%fused_computation.20 | convolution fusion | flops 648130560 | bytes 5349888 | tf_op jit(solution)/shard_map/while/body/fks,fmk->fms/dot_general | solution.py:57
  84.8 8.4 %all-reduce.1 = bf16[8,128,411]{1,2,0:T(8,128)(2,1)} all-reduce(f32[8,128,411]{1,2,0:T(8,128)S(1)} %fusion.8), channel_id=1, replica_groups=mesh['tile'=128,'chan'=2] {'chan'}, use_global_device_ids=true, to_apply=%region_2.4 | all-reduce | flops 420864 | bytes 2525184 | tf_op jit(solution)/shard_map/while/body/psum | solution.py:60
  93.3 1.4 copy.27
  94.7 1.1 broadcast_in_dim.60
  95.8 2.0 %while.16 = (s32[]{:T(128)}, bf16[8,128,411]{2,1,0:T(8,128)(2,1)}, s32[]{:T(128)}, s32[]{:T(128)}, bf16[8,128,411]{2,1,0:T(8,128)(2,1)S(1)}, /*index=5*/s32[]{:T(128)}, s32[]{:T(128)}) while((s32[]{:T(128)}, bf16[8,128,411]{2,1,0:T(8,128)(2,1)}, s32[]{:T(128)}, s32[]{:T(128)}, bf16[8,128,411]{2,1,0:T(8,128)(2,1)S(1)}, /*index=5*/s32[]{:T(128)}, ...), condition=%wide.region_4.6_spmd, body=%wide.region_3.5_spmd.sunk | while | flops 420883 | bytes 1683569 | solution.py:65
  95.8 0.7 add_compare_fusion.2
  96.4 1.3 select_convert_fusion.2
  97.8 2.6 %reshape.37 = bf16[8,52608]{1,0:T(8,128)(2,1)S(1)} reshape(bf16[8,128,411]{2,1,0:T(8,128)(2,1)} %get-tuple-element.179) | data formatting | bytes 1683456 | tf_op jit(solution)/shard_map/reshape | solution.py:66
  100.4 0.7 convolution_convert_fusion.1
  101.1 0.7 fusion.21
  101.8 1.1 collective-permute-start.6
  102.9 1.2 collective-permute-start.7
  104.1 4.2 %collective-permute-start.8 = (bf16[3,52608]{1,0:T(4,128)(2,1)S(1)}, bf16[3,52608]{1,0:T(4,128)(2,1)S(1)}, u32[]{:S(2)}, u32[]{:S(2)}) collective-permute-start(bf16[3,52608]{1,0:T(4,128)(2,1)S(1)} %get-tuple-element.215), channel_id=1, source_target_pairs={{0,4},{2,6},{4,8},{6,10},{8,12},{10,14},{12,16},{14,18},{16,20},{1... | collective-permute-start | bytes 946952 | tf_op jit(solution)/shard_map/ppermute | solution.py:13
  108.3 0.1 pad_add_fusion
  108.4 5.5 %collective-permute-done.6 = bf16[3,52608]{1,0:T(4,128)(2,1)S(1)} collective-permute-done((bf16[3,52608]{1,0:T(4,128)(2,1)S(1)}, bf16[3,52608]{1,0:T(4,128)(2,1)S(1)}, u32[]{:S(2)}, u32[]{:S(2)}) %collective-permute-start.6) | collective-permute-done | bytes 315680 | tf_op jit(solution)/shard_map/ppermute | solution.py:13
  113.9 6.9 %collective-permute-done.7 = bf16[3,52608]{1,0:T(4,128)(2,1)S(1)} collective-permute-done((bf16[3,52608]{1,0:T(4,128)(2,1)S(1)}, bf16[3,52608]{1,0:T(4,128)(2,1)S(1)}, u32[]{:S(2)}, u32[]{:S(2)}) %collective-permute-start.7) | collective-permute-done | bytes 315680 | tf_op jit(solution)/shard_map/ppermute | solution.py:13
  120.8 19.4 %collective-permute-done.8 = bf16[3,52608]{1,0:T(4,128)(2,1)S(1)} collective-permute-done((bf16[3,52608]{1,0:T(4,128)(2,1)S(1)}, bf16[3,52608]{1,0:T(4,128)(2,1)S(1)}, u32[]{:S(2)}, u32[]{:S(2)}) %collective-permute-start.8) | collective-permute-done | bytes 315680 | tf_op jit(solution)/shard_map/ppermute | solution.py:13
  140.2 1.4 convolution_convert_fusion
  141.6 5.0 %reshape.38 = bf16[16,128,411]{2,1,0:T(8,128)(2,1)} reshape(bf16[16,52608]{1,0:T(8,128)(2,1)S(1)} %convolution_convert_fusion) | data formatting | bytes 3366912 | tf_op jit(solution)/shard_map/reshape | solution.py:88
  146.6 4.3 %copy.28 = bf16[16,128,411]{1,0,2:T(8,128)(2,1)} copy(bf16[16,128,411]{2,1,0:T(8,128)(2,1)} %reshape.38) | data formatting | bytes 3366912 | tf_op jit(solution)/shard_map/reshape | solution.py:88
  (12 shorter events, 0.1 us)
Async XLA Ops:
  6.5 14.2 %copy-start = (bf16[16,128,411]{1,0,2:T(8,128)(2,1)S(1)}, bf16[16,128,411]{1,0,2:T(8,128)(2,1)}, u32[]{:S(2)}) copy-start(bf16[16,128,411]{1,0,2:T(8,128)(2,1)} %param.14) | copy-start | bytes 5050372
  6.5 74.7 %all-gather.2.cloned.1.call-start = ((), (), s32[]{:S(2)}) async-start(), calls=%async_computation | async-start | bytes 1892352 | tf_op jit(solution)/shard_map/while/body/all_gather | solution.py:52
  9.0 14.2 %collective-permute-start = (s32[3]{0:T(128)S(1)}, s32[3]{0:T(128)S(1)}, u32[]{:S(2)}, u32[]{:S(2)}) collective-permute-start(s32[3]{0:T(128)S(1)} %get-tuple-element.221), channel_id=1, source_target_pairs={{0,254},{2,0},{4,2},{6,4},{8,6},{10,8},{12,10},{14,12},{16,14},{18... | collective-permute-start | bytes 44 | tf_op jit(solution)/shard_map/ppermute | solution.py:13
  11.2 15.6 %collective-permute-start.1 = (s32[3]{0:T(128)S(1)}, s32[3]{0:T(128)S(1)}, u32[]{:S(2)}, u32[]{:S(2)}) collective-permute-start(s32[3]{0:T(128)S(1)} %get-tuple-element.220), channel_id=1, source_target_pairs={{0,2},{2,4},{4,6},{6,8},{8,10},{10,12},{12,14},{14,16},{16,18},{18... | collective-permute-start | bytes 44 | tf_op jit(solution)/shard_map/ppermute | solution.py:13
  11.2 23.6 %collective-permute-start.2 = (s32[3]{0:T(128)S(1)}, s32[3]{0:T(128)S(1)}, u32[]{:S(2)}, u32[]{:S(2)}) collective-permute-start(s32[3]{0:T(128)S(1)} %get-tuple-element.219), channel_id=1, source_target_pairs={{0,4},{2,6},{4,8},{6,10},{8,12},{10,14},{12,16},{14,18},{16,20},{1... | collective-permute-start | bytes 44 | tf_op jit(solution)/shard_map/ppermute | solution.py:13
  16.2 4.6 %copy-start.1 = (bf16[8,308]{1,0:T(8,128)(2,1)S(1)}, bf16[8,308]{1,0:T(8,128)(2,1)}, u32[]{:S(2)}) copy-start(bf16[8,308]{1,0:T(8,128)(2,1)} %param.13) | copy-start | bytes 14788
  26.8 19.4 %collective-permute-start.3 = (bf16[3,128,411]{1,0,2:T(4,128)(2,1)}, bf16[3,128,411]{1,0,2:T(4,128)(2,1)S(1)}, u32[]{:S(2)}, u32[]{:S(2)}) collective-permute-start(bf16[3,128,411]{1,0,2:T(4,128)(2,1)} %broadcast_select_fusion.3), channel_id=1, source_target_pairs={{0,2},{2,4},{4,6},{6,8},{8,10},{10,12},{12,14},{14,16},{16,18},{18... | collective-permute-start | bytes 946952 | tf_op jit(solution)/shard_map/ppermute | solution.py:13
  30.3 22.5 %collective-permute-start.4 = (bf16[3,128,411]{1,0,2:T(4,128)(2,1)}, bf16[3,128,411]{1,0,2:T(4,128)(2,1)S(1)}, u32[]{:S(2)}, u32[]{:S(2)}) collective-permute-start(bf16[3,128,411]{1,0,2:T(4,128)(2,1)} %broadcast_select_fusion.1), channel_id=1, source_target_pairs={{0,254},{2,0},{4,2},{6,4},{8,6},{10,8},{12,10},{14,12},{16,14},{18... | collective-permute-start | bytes 946952 | tf_op jit(solution)/shard_map/ppermute | solution.py:13
  37.5 19.9 %collective-permute-start.5 = (bf16[3,128,411]{1,0,2:T(4,128)(2,1)S(1)}, bf16[3,128,411]{1,0,2:T(4,128)(2,1)S(1)}, u32[]{:S(2)}, u32[]{:S(2)}) collective-permute-start(bf16[3,128,411]{1,0,2:T(4,128)(2,1)S(1)} %broadcast_select_fusion), channel_id=1, source_target_pairs={{0,252},{2,254},{4,0},{6,2},{8,4},{10,6},{12,8},{14,10},{16,12},{1... | collective-permute-start | bytes 946952 | tf_op jit(solution)/shard_map/ppermute | solution.py:13
  101.8 12.1 %collective-permute-start.6 = (bf16[3,52608]{1,0:T(4,128)(2,1)S(1)}, bf16[3,52608]{1,0:T(4,128)(2,1)S(1)}, u32[]{:S(2)}, u32[]{:S(2)}) collective-permute-start(bf16[3,52608]{1,0:T(4,128)(2,1)S(1)} %get-tuple-element.214), channel_id=1, source_target_pairs={{0,254},{2,0},{4,2},{6,4},{8,6},{10,8},{12,10},{14,12},{16,14},{18... | collective-permute-start | bytes 946952 | tf_op jit(solution)/shard_map/ppermute | solution.py:13
  102.9 17.9 %collective-permute-start.7 = (bf16[3,52608]{1,0:T(4,128)(2,1)S(1)}, bf16[3,52608]{1,0:T(4,128)(2,1)S(1)}, u32[]{:S(2)}, u32[]{:S(2)}) collective-permute-start(bf16[3,52608]{1,0:T(4,128)(2,1)S(1)} %get-tuple-element.216), channel_id=1, source_target_pairs={{0,2},{2,4},{4,6},{6,8},{8,10},{10,12},{12,14},{14,16},{16,18},{18... | collective-permute-start | bytes 946952 | tf_op jit(solution)/shard_map/ppermute | solution.py:13
  104.1 36.1 %collective-permute-start.8 = (bf16[3,52608]{1,0:T(4,128)(2,1)S(1)}, bf16[3,52608]{1,0:T(4,128)(2,1)S(1)}, u32[]{:S(2)}, u32[]{:S(2)}) collective-permute-start(bf16[3,52608]{1,0:T(4,128)(2,1)S(1)} %get-tuple-element.215), channel_id=1, source_target_pairs={{0,4},{2,6},{4,8},{6,10},{8,12},{10,14},{12,16},{14,18},{16,20},{1... | collective-permute-start | bytes 946952 | tf_op jit(solution)/shard_map/ppermute | solution.py:13
Sparse Core Ops, SparseCore 0:
  65.1 16.1 all-gather.1
where the time goes:
time: 158 us
  waiting for transfers between devices  58.7 us (37%)
  local copies, waits for them, and re-layouts  32.4 us (21%)
  starting transfers between devices  25.9 us (16%)
  between operations  14.2 us (9%)
  other arithmetic  9.06 us (6%)
  matrix products  9.01 us (6%)
  blocking collectives  8.43 us (5%)
    ppermute x9, waiting for transfers between devices, passed_along(): lax.ppermute(value, axis, [(i, (i + by) % count) for i in range(count)])  43.1 us
    ppermute x9, starting transfers between devices, passed_along(): lax.ppermute(value, axis, [(i, (i + by) % count) for i in range(count)])  25.9 us
    all_gather x1, waiting for transfers between devices, one_block(): all_channels = lax.all_gather(departure, 'chan', axis=2, tiled=True)  15.6 us
    reshape x2, local copies, waits for them, and re-layouts, on_device(): gradient = gradient.reshape(columns, members, state)  9.34 us
    psum x1, blocking collectives, one_block(): summed = lax.psum(partial_adj, 'chan')  8.43 us
    gather x3, local copies, waits for them, and re-layouts, on_device(): picked = jnp.take(increments, asked, axis=0)  7.38 us
    unnamed x5, local copies, waits for them, and re-layouts  4.56 us
    dot_general x1, matrix products, one_block(): jnp.einsum('fks,fmk->fms', jac_all, weighted, preferred_element_type=jnp....  3.6 us
  transfers between devices with their start and end apart: 10, of which 6 were waited for; matrix products, arithmetic and copies ran while one was open for 11% of the time, Pallas kernels for 0%

commit v1 on v0

--- a/solution.py
+++ b/solution.py
@@ -57,7 +57,7 @@
         partial_adj = jnp.einsum(
             "fks,fmk->fms", jac_all, weighted, preferred_element_type=jnp.float32
         )
-        summed = lax.psum(partial_adj, "chan")
+        summed = jnp.sum(lax.all_gather(partial_adj, "chan"), axis=0)
         live = start + jnp.arange(group_rows, dtype=jnp.int32) < count
         summed = jnp.where(live[:, None, None], summed, jnp.zeros_like(summed)).astype(jnp.bfloat16)
         return summed

time: 158 us -> 174 us (1.10)
  waiting for transfers between devices: 58.7 us -> 77.3 us
  blocking collectives: 8.43 us -> 0 us
  other arithmetic: 9.06 us -> 12.4 us
  local copies, waits for them, and re-layouts: 32.4 us -> 34.7 us
    all_gather x0 -> x1, waiting for transfers between devices: none -> 17.9 us  [one_block(): summed = jnp.sum(lax.all_gather(partial_adj, 'chan'), axis=0)]
    psum x1 -> x0, blocking collectives: 8.43 us -> none  [one_block(): summed = lax.psum(partial_adj, 'chan')]
    reduce_sum x0 -> x1, other arithmetic: none -> 3.34 us  [one_block(): summed = jnp.sum(lax.all_gather(partial_adj, 'chan'), axis=0)]
    dot_general x0 -> x1, local copies, waits for them, and re-layouts: none -> 2.16 us  [one_block(): jnp.einsum('fks,fmk->fms', jac_all, weighted, preferred_element_type=jnp....]
  transfers between devices with their start and end apart: 10 -> 11, of which waited for: 6 -> 7; matrix products, arithmetic and copies ran while one was open for 11% -> 10% of each run, Pallas kernels for 0% -> 0%
where the time goes in v1:
time: 174 us; the launch traced here: 173 us
  waiting for transfers between devices  77.3 us (44%)
  local copies, waits for them, and re-layouts  34.7 us (20%)
  starting transfers between devices  25.7 us (15%)
  between operations  14.3 us (8%)
  other arithmetic  12.4 us (7%)
  matrix products  9.01 us (5%)
    ppermute x9, waiting for transfers between devices, passed_along(): lax.ppermute(value, axis, [(i, (i + by) % count) for i in range(count)])  43.1 us
    ppermute x9, starting transfers between devices, passed_along(): lax.ppermute(value, axis, [(i, (i + by) % count) for i in range(count)])  25.7 us
    all_gather x1, waiting for transfers between devices, one_block(): summed = jnp.sum(lax.all_gather(partial_adj, 'chan'), axis=0)  17.9 us
    all_gather x1, waiting for transfers between devices, one_block(): all_channels = lax.all_gather(departure, 'chan', axis=2, tiled=True)  16.2 us
    reshape x2, local copies, waits for them, and re-layouts, on_device(): gradient = gradient.reshape(columns, members, state)  9.32 us
    gather x3, local copies, waits for them, and re-layouts, on_device(): picked = jnp.take(increments, asked, axis=0)  7.38 us
    unnamed x5, local copies, waits for them, and re-layouts  4.55 us
    dot_general x1, matrix products, one_block(): jnp.einsum('fks,fmk->fms', jac_all, weighted, preferred_element_type=jnp....  3.6 us
  transfers between devices with their start and end apart: 11, of which 7 were waited for; matrix products, arithmetic and copies ran while one was open for 10% of the time, Pallas kernels for 0%

profile of v1, /device:TPU:8, one launch (start us, length us, event | category | flops | bytes accessed | tf_op | source)
XLA Modules:
  0.0 173.4 jit_solution(12073533205643594312)
XLA Ops:
  6.5 0.0 copy-start
  6.5 0.0 all-gather.4.cloned.1.call-start
  6.5 1.0 convert_reduce_fusion
  7.5 0.7 multiply_add_fusion
  8.2 0.7 select_reduce_fusion
  8.9 0.1 fusion.22
  9.0 2.2 %collective-permute-start = (s32[3]{0:T(128)S(1)}, s32[3]{0:T(128)S(1)}, u32[]{:S(2)}, u32[]{:S(2)}) collective-permute-start(s32[3]{0:T(128)S(1)} %get-tuple-element.178), channel_id=1, source_target_pairs={{0,254},{2,0},{4,2},{6,4},{8,6},{10,8},{12,10},{14,12},{16,14},{18... | collective-permute-start | bytes 44 | tf_op jit(solution)/shard_map/ppermute | solution.py:13
  11.2 0.0 collective-permute-start.1
  11.2 4.3 %collective-permute-start.2 = (s32[3]{0:T(128)S(1)}, s32[3]{0:T(128)S(1)}, u32[]{:S(2)}, u32[]{:S(2)}) collective-permute-start(s32[3]{0:T(128)S(1)} %get-tuple-element.176), channel_id=1, source_target_pairs={{0,4},{2,6},{4,8},{6,10},{8,12},{10,14},{12,16},{14,18},{16,20},{1... | collective-permute-start | bytes 44 | tf_op jit(solution)/shard_map/ppermute | solution.py:13
  15.4 0.1 compare_and_fusion.2
  15.5 0.7 and_bitcast_fusion
  16.2 0.0 copy-start.1
  16.2 4.5 %copy.26 = bf16[8,308,411]{1,2,0:T(8,128)(2,1)} copy(bf16[8,308,411]{2,0,1:T(8,128)(2,1)} %param.11) | data formatting | bytes 4050816 | tf_op args[0]
  20.7 0.0 copy-done.1
  20.7 0.0 copy-done
  20.7 2.5 %gather_fusion.2 = bf16[3,128,411]{1,0,2:T(4,128)(2,1)S(1)} fusion(bf16[16,128,411]{1,0,2:T(8,128)(2,1)S(1)} %copy-done, s32[1024]{0:T(1024)S(1)} %pad_clamp_fusion.3), kind=kCustom, calls=%fused_computation.1.clone | custom fusion | bytes 631308 | tf_op jit(solution)/shard_map/jit(_take)/gather | solution.py:35
  23.2 0.0 collective-permute-done
  23.2 2.5 %gather_fusion.1 = bf16[3,128,411]{1,0,2:T(4,128)(2,1)S(1)} fusion(bf16[16,128,411]{1,0,2:T(8,128)(2,1)S(1)} %copy-done, s32[1024]{0:T(1024)S(1)} %pad_clamp_fusion.4), kind=kCustom, calls=%fused_computation.clone | custom fusion | bytes 631308 | tf_op jit(solution)/shard_map/jit(_take)/gather | solution.py:38
  25.7 1.0 broadcast_select_fusion.3
  26.7 0.0 collective-permute-start.3
  26.8 0.0 collective-permute-done.1
  26.8 2.5 %gather_fusion.3 = bf16[3,128,411]{1,0,2:T(4,128)(2,1)S(1)} fusion(bf16[16,128,411]{1,0,2:T(8,128)(2,1)S(1)} %copy-done, s32[1024]{0:T(1024)S(1)} %pad_clamp_fusion.2), kind=kCustom, calls=%fused_computation.2.clone | custom fusion | bytes 631308 | tf_op jit(solution)/shard_map/jit(_take)/gather | solution.py:38
  29.3 1.0 broadcast_select_fusion.1
  30.2 4.5 %collective-permute-start.4 = (bf16[3,128,411]{1,0,2:T(4,128)(2,1)}, bf16[3,128,411]{1,0,2:T(4,128)(2,1)S(1)}, u32[]{:S(2)}, u32[]{:S(2)}) collective-permute-start(bf16[3,128,411]{1,0,2:T(4,128)(2,1)} %broadcast_select_fusion.1), channel_id=1, source_target_pairs={{0,254},{2,0},{4,2},{6,4},{8,6},{10,8},{12,10},{14,12},{16,14},{18... | collective-permute-start | bytes 946952 | tf_op jit(solution)/shard_map/ppermute | solution.py:13
  34.8 0.0 collective-permute-done.2
  34.8 2.5 %gather_fusion.4 = bf16[3,128,411]{1,0,2:T(4,128)(2,1)S(1)} fusion(bf16[16,128,411]{1,0,2:T(8,128)(2,1)S(1)} %copy-done, s32[1024]{0:T(1024)S(1)} %pad_clamp_fusion.1), kind=kCustom, calls=%fused_computation.3.clone | custom fusion | bytes 631308 | tf_op jit(solution)/shard_map/jit(_take)/gather | solution.py:38
  37.3 0.2 broadcast_select_fusion
  37.5 8.4 %collective-permute-start.5 = (bf16[3,128,411]{1,0,2:T(4,128)(2,1)S(1)}, bf16[3,128,411]{1,0,2:T(4,128)(2,1)S(1)}, u32[]{:S(2)}, u32[]{:S(2)}) collective-permute-start(bf16[3,128,411]{1,0,2:T(4,128)(2,1)S(1)} %broadcast_select_fusion), channel_id=1, source_target_pairs={{0,252},{2,254},{4,0},{6,2},{8,4},{10,6},{12,8},{14,10},{16,12},{1... | collective-permute-start | bytes 946952 | tf_op jit(solution)/shard_map/ppermute | solution.py:13
  45.9 0.2 broadcast_select_fusion.2
  46.1 0.0 collective-permute-done.3
  46.1 6.7 %collective-permute-done.4 = bf16[3,128,411]{1,0,2:T(4,128)(2,1)S(1)} collective-permute-done((bf16[3,128,411]{1,0,2:T(4,128)(2,1)}, bf16[3,128,411]{1,0,2:T(4,128)(2,1)S(1)}, u32[]{:S(2)}, u32[]{:S(2)}) %collective-permute-start.4) | collective-permute-done | bytes 315680 | tf_op jit(solution)/shard_map/ppermute | solution.py:13
  52.8 4.7 %collective-permute-done.5 = bf16[3,128,411]{1,0,2:T(4,128)(2,1)S(1)} collective-permute-done((bf16[3,128,411]{1,0,2:T(4,128)(2,1)S(1)}, bf16[3,128,411]{1,0,2:T(4,128)(2,1)S(1)}, u32[]{:S(2)}, u32[]{:S(2)}) %collective-permute-start.5) | collective-permute-done | bytes 315680 | tf_op jit(solution)/shard_map/ppermute | solution.py:13
  57.5 1.4 pad_maximum_fusion
  58.8 0.3 copy.22
  59.1 1.6 gather_fusion
  60.7 3.3 %fusion.7 = bf16[8,128,308]{1,2,0:T(8,128)(2,1)S(1)} fusion(bf16[8,308,411]{1,2,0:T(8,128)(2,1)} %copy.26, bf16[8,128,411]{1,2,0:T(8,128)(2,1)} %gather_fusion, pred[8]{0:T(512)(128)(4,1)S(1)} %get-tuple-element.167, f32[8,308]{1,0:T(8,128)S(1)} %convert_element_type.44), kind=kOutput, calls=%fused_computation.19 | convolution fusion | flops 260303872 | bytes 3507784 | tf_op jit(solution)/shard_map/while/body/fks,fms->fmk/dot_general | solution.py:48
  64.0 0.9 copy.24
  64.9 0.0 all-gather.4.cloned.1.call-update
  64.9 0.0 all-gather.6.cloned.1.call-start
  65.0 16.2 %all-gather.4.cloned.1.call-done = bf16[8,128,616]{1,0,2:T(8,128)(2,1)} async-done(((bf16[8,128,308]{1,0,2:T(8,128)(2,1)}), bf16[8,128,616]{1,0,2:T(8,128)(2,1)}) %all-gather.4.cloned.1.call-update) | async-done | bytes 1261584 | tf_op jit(solution)/shard_map/while/body/all_gather | solution.py:52
  81.2 3.6 %fusion.8 = f32[8,128,411]{1,2,0:T(8,128)S(1)} fusion(bf16[8,308,411]{1,2,0:T(8,128)(2,1)} %copy.26, bf16[8,128,616]{1,0,2:T(8,128)(2,1)} %all-gather.4.cloned.1.call-done, bf16[308,616]{1,0:T(8,128)(2,1)} %param.12), kind=kOutput, calls=%fused_computation.21 | convolution fusion | flops 648130560 | bytes 5349888 | tf_op jit(solution)/shard_map/while/body/fks,fmk->fms/dot_general | solution.py:57
  84.8 2.2 %copy.27 = f32[8,128,411]{1,0,2:T(8,128)} copy(f32[8,128,411]{1,2,0:T(8,128)S(1)} %fusion.8) | data formatting | bytes 3366912 | tf_op jit(solution)/shard_map/while/body/fks,fmk->fms/dot_general | solution.py:57
  87.0 0.0 all-gather.6.cloned.1.call-update
  87.7 17.9 %all-gather.6.cloned.1.call-done = f32[16,128,411]{1,0,2:T(8,128)} async-done(((f32[8,128,411]{1,0,2:T(8,128)}), f32[16,128,411]{1,0,2:T(8,128)}) %all-gather.6.cloned.1.call-update) | async-done | bytes 3366928 | tf_op jit(solution)/shard_map/while/body/all_gather | solution.py:60
  105.5 3.3 %bitcast_reduce_fusion = bf16[8,128,411]{1,0,2:T(8,128)(2,1)} fusion(f32[16,128,411]{1,0,2:T(8,128)} %all-gather.6.cloned.1.call-done), kind=kLoop, calls=%fused_computation.9 | loop fusion | flops 420864 | bytes 4208640 | tf_op jit(solution)/shard_map/while/body/reduce_sum | solution.py:60
  108.9 1.6 copy.29
  110.5 1.1 broadcast_in_dim.58
  111.6 2.0 %while.14 = (s32[]{:T(128)}, bf16[8,128,411]{2,1,0:T(8,128)(2,1)}, s32[]{:T(128)}, s32[]{:T(128)}, bf16[8,128,411]{2,1,0:T(8,128)(2,1)S(1)}, /*index=5*/s32[]{:T(128)}, s32[]{:T(128)}) while((s32[]{:T(128)}, bf16[8,128,411]{2,1,0:T(8,128)(2,1)}, s32[]{:T(128)}, s32[]{:T(128)}, bf16[8,128,411]{2,1,0:T(8,128)(2,1)S(1)}, /*index=5*/s32[]{:T(128)}, ...), condition=%wide.region_4.6_spmd, body=%wide.region_3.5_spmd.sunk | while | flops 420883 | bytes 1683569 | solution.py:65
  111.6 0.7 add_compare_fusion.2
  112.2 1.3 select_convert_fusion.2
  113.6 2.6 %reshape.37 = bf16[8,52608]{1,0:T(8,128)(2,1)S(1)} reshape(bf16[8,128,411]{2,1,0:T(8,128)(2,1)} %get-tuple-element.146) | data formatting | bytes 1683456 | tf_op jit(solution)/shard_map/reshape | solution.py:66
  116.2 0.7 convolution_convert_fusion.1
  116.9 0.7 fusion.21
  117.6 0.9 collective-permute-start.6
  118.4 1.2 collective-permute-start.7
  119.7 4.2 %collective-permute-start.8 = (bf16[3,52608]{1,0:T(4,128)(2,1)S(1)}, bf16[3,52608]{1,0:T(4,128)(2,1)S(1)}, u32[]{:S(2)}, u32[]{:S(2)}) collective-permute-start(bf16[3,52608]{1,0:T(4,128)(2,1)S(1)} %get-tuple-element.172), channel_id=1, source_target_pairs={{0,4},{2,6},{4,8},{6,10},{8,12},{10,14},{12,16},{14,18},{16,20},{1... | collective-permute-start | bytes 946952 | tf_op jit(solution)/shard_map/ppermute | solution.py:13
  123.9 0.1 pad_add_fusion
  124.0 5.5 %collective-permute-done.6 = bf16[3,52608]{1,0:T(4,128)(2,1)S(1)} collective-permute-done((bf16[3,52608]{1,0:T(4,128)(2,1)S(1)}, bf16[3,52608]{1,0:T(4,128)(2,1)S(1)}, u32[]{:S(2)}, u32[]{:S(2)}) %collective-permute-start.6) | collective-permute-done | bytes 315680 | tf_op jit(solution)/shard_map/ppermute | solution.py:13
  129.5 6.8 %collective-permute-done.7 = bf16[3,52608]{1,0:T(4,128)(2,1)S(1)} collective-permute-done((bf16[3,52608]{1,0:T(4,128)(2,1)S(1)}, bf16[3,52608]{1,0:T(4,128)(2,1)S(1)}, u32[]{:S(2)}, u32[]{:S(2)}) %collective-permute-start.7) | collective-permute-done | bytes 315680 | tf_op jit(solution)/shard_map/ppermute | solution.py:13
  136.4 19.4 %collective-permute-done.8 = bf16[3,52608]{1,0:T(4,128)(2,1)S(1)} collective-permute-done((bf16[3,52608]{1,0:T(4,128)(2,1)S(1)}, bf16[3,52608]{1,0:T(4,128)(2,1)S(1)}, u32[]{:S(2)}, u32[]{:S(2)}) %collective-permute-start.8) | collective-permute-done | bytes 315680 | tf_op jit(solution)/shard_map/ppermute | solution.py:13
  155.8 1.4 convolution_convert_fusion
  157.2 5.0 %reshape.38 = bf16[16,128,411]{2,1,0:T(8,128)(2,1)} reshape(bf16[16,52608]{1,0:T(8,128)(2,1)S(1)} %convolution_convert_fusion) | data formatting | bytes 3366912 | tf_op jit(solution)/shard_map/reshape | solution.py:88
  162.2 4.3 %copy.30 = bf16[16,128,411]{1,0,2:T(8,128)(2,1)} copy(bf16[16,128,411]{2,1,0:T(8,128)(2,1)} %reshape.38) | data formatting | bytes 3366912 | tf_op jit(solution)/shard_map/reshape | solution.py:88
  (12 shorter events, 0.1 us)
Async XLA Ops:
  6.5 14.2 %copy-start = (bf16[16,128,411]{1,0,2:T(8,128)(2,1)S(1)}, bf16[16,128,411]{1,0,2:T(8,128)(2,1)}, u32[]{:S(2)}) copy-start(bf16[16,128,411]{1,0,2:T(8,128)(2,1)} %param.14) | copy-start | bytes 5050372
  6.5 74.7 %all-gather.4.cloned.1.call-start = ((), (), s32[]{:S(2)}) async-start(), calls=%async_computation | async-start | bytes 1892352 | tf_op jit(solution)/shard_map/while/body/all_gather | solution.py:52
  9.0 14.2 %collective-permute-start = (s32[3]{0:T(128)S(1)}, s32[3]{0:T(128)S(1)}, u32[]{:S(2)}, u32[]{:S(2)}) collective-permute-start(s32[3]{0:T(128)S(1)} %get-tuple-element.178), channel_id=1, source_target_pairs={{0,254},{2,0},{4,2},{6,4},{8,6},{10,8},{12,10},{14,12},{16,14},{18... | collective-permute-start | bytes 44 | tf_op jit(solution)/shard_map/ppermute | solution.py:13
  11.2 15.6 %collective-permute-start.1 = (s32[3]{0:T(128)S(1)}, s32[3]{0:T(128)S(1)}, u32[]{:S(2)}, u32[]{:S(2)}) collective-permute-start(s32[3]{0:T(128)S(1)} %get-tuple-element.177), channel_id=1, source_target_pairs={{0,2},{2,4},{4,6},{6,8},{8,10},{10,12},{12,14},{14,16},{16,18},{18... | collective-permute-start | bytes 44 | tf_op jit(solution)/shard_map/ppermute | solution.py:13
  11.2 23.6 %collective-permute-start.2 = (s32[3]{0:T(128)S(1)}, s32[3]{0:T(128)S(1)}, u32[]{:S(2)}, u32[]{:S(2)}) collective-permute-start(s32[3]{0:T(128)S(1)} %get-tuple-element.176), channel_id=1, source_target_pairs={{0,4},{2,6},{4,8},{6,10},{8,12},{10,14},{12,16},{14,18},{16,20},{1... | collective-permute-start | bytes 44 | tf_op jit(solution)/shard_map/ppermute | solution.py:13
  16.2 4.6 %copy-start.1 = (bf16[8,308]{1,0:T(8,128)(2,1)S(1)}, bf16[8,308]{1,0:T(8,128)(2,1)}, u32[]{:S(2)}) copy-start(bf16[8,308]{1,0:T(8,128)(2,1)} %param.13) | copy-start | bytes 14788
  26.7 19.4 %collective-permute-start.3 = (bf16[3,128,411]{1,0,2:T(4,128)(2,1)}, bf16[3,128,411]{1,0,2:T(4,128)(2,1)S(1)}, u32[]{:S(2)}, u32[]{:S(2)}) collective-permute-start(bf16[3,128,411]{1,0,2:T(4,128)(2,1)} %broadcast_select_fusion.3), channel_id=1, source_target_pairs={{0,2},{2,4},{4,6},{6,8},{8,10},{10,12},{12,14},{14,16},{16,18},{18... | collective-permute-start | bytes 946952 | tf_op jit(solution)/shard_map/ppermute | solution.py:13
  30.2 22.5 %collective-permute-start.4 = (bf16[3,128,411]{1,0,2:T(4,128)(2,1)}, bf16[3,128,411]{1,0,2:T(4,128)(2,1)S(1)}, u32[]{:S(2)}, u32[]{:S(2)}) collective-permute-start(bf16[3,128,411]{1,0,2:T(4,128)(2,1)} %broadcast_select_fusion.1), channel_id=1, source_target_pairs={{0,254},{2,0},{4,2},{6,4},{8,6},{10,8},{12,10},{14,12},{16,14},{18... | collective-permute-start | bytes 946952 | tf_op jit(solution)/shard_map/ppermute | solution.py:13
  37.5 19.9 %collective-permute-start.5 = (bf16[3,128,411]{1,0,2:T(4,128)(2,1)S(1)}, bf16[3,128,411]{1,0,2:T(4,128)(2,1)S(1)}, u32[]{:S(2)}, u32[]{:S(2)}) collective-permute-start(bf16[3,128,411]{1,0,2:T(4,128)(2,1)S(1)} %broadcast_select_fusion), channel_id=1, source_target_pairs={{0,252},{2,254},{4,0},{6,2},{8,4},{10,6},{12,8},{14,10},{16,12},{1... | collective-permute-start | bytes 946952 | tf_op jit(solution)/shard_map/ppermute | solution.py:13
  64.9 40.6 %all-gather.6.cloned.1.call-start = ((), (), s32[]{:S(2)}) async-start(), calls=%async_computation.1 | async-start | bytes 5050368 | tf_op jit(solution)/shard_map/while/body/all_gather | solution.py:60
  117.6 12.0 %collective-permute-start.6 = (bf16[3,52608]{1,0:T(4,128)(2,1)S(1)}, bf16[3,52608]{1,0:T(4,128)(2,1)S(1)}, u32[]{:S(2)}, u32[]{:S(2)}) collective-permute-start(bf16[3,52608]{1,0:T(4,128)(2,1)S(1)} %get-tuple-element.171), channel_id=1, source_target_pairs={{0,254},{2,0},{4,2},{6,4},{8,6},{10,8},{12,10},{14,12},{16,14},{18... | collective-permute-start | bytes 946952 | tf_op jit(solution)/shard_map/ppermute | solution.py:13
  118.4 17.9 %collective-permute-start.7 = (bf16[3,52608]{1,0:T(4,128)(2,1)S(1)}, bf16[3,52608]{1,0:T(4,128)(2,1)S(1)}, u32[]{:S(2)}, u32[]{:S(2)}) collective-permute-start(bf16[3,52608]{1,0:T(4,128)(2,1)S(1)} %get-tuple-element.173), channel_id=1, source_target_pairs={{0,2},{2,4},{4,6},{6,8},{8,10},{10,12},{12,14},{14,16},{16,18},{18... | collective-permute-start | bytes 946952 | tf_op jit(solution)/shard_map/ppermute | solution.py:13
  119.7 36.1 %collective-permute-start.8 = (bf16[3,52608]{1,0:T(4,128)(2,1)S(1)}, bf16[3,52608]{1,0:T(4,128)(2,1)S(1)}, u32[]{:S(2)}, u32[]{:S(2)}) collective-permute-start(bf16[3,52608]{1,0:T(4,128)(2,1)S(1)} %get-tuple-element.172), channel_id=1, source_target_pairs={{0,4},{2,6},{4,8},{6,10},{8,12},{10,14},{12,16},{14,18},{16,20},{1... | collective-permute-start | bytes 946952 | tf_op jit(solution)/shard_map/ppermute | solution.py:13
Sparse Core Ops, SparseCore 0:
  65.1 16.1 all-gather.3
  87.1 18.3 all-gather.5
